TPU v7x, 512 devices: a whole 4x8x8 slice. The times are simulated.
512 devices in a mesh: dp: 16 (over z, core), mp: 32 (over x, y).
Axes of the slice: x: 4, y: 8, z: 8, core: 2. Of those that a mesh axis runs over, the one named last changes fastest.
Arguments:
- tokens: bfloat16 [2048, 4096], P(('dp', 'mp')), may hold values from -6 to 6
- hidden_grad: bfloat16 [2048, 14336], P('dp', 'mp'), may hold values from -0.125 to 0.125
- gate_weight: bfloat16 [4096, 14336], P('dp', 'mp'), may hold values from -0.09375 to 0.09375
- up_weight: bfloat16 [4096, 14336], P('dp', 'mp'), may hold values from -0.09375 to 0.09375
- gate_probe: bfloat16 [4096, 14336], P('dp', 'mp'), may hold values from -1 to 1, as said below
- gate_mean: float32 [4096, 14336], P('dp', 'mp'), may hold values from -0.6 to 0.6
- gate_curve: float32 [4096, 14336], P('dp', 'mp'), may hold values from 1 to 10
- group_counts: int32 [16], replicated, may hold values from 32 to 128, as said below
Outputs:
- gate_weight_new: bfloat16 [4096, 14336], P('dp', 'mp')
- gate_mean_new: float32 [4096, 14336], P('dp', 'mp')
- gate_curve_new: float32 [4096, 14336], P('dp', 'mp')
Inputs may be any that keep to these rules, and one draw needn't show every extreme that they name: `group_counts`: some data group has exactly 128 live tokens in every draw. `gate_probe`: every entry is -1 or 1, each sign drawn independently.
All inputs are finite; a program needn't handle non-finite values.
Results may differ from a plain program's by a relative error of at most 0.0017.
Values may be sent and summed in bfloat16 or wider, within the bound.
No kernel may reach another device: no remote copies, remote signals or barrier semaphores. Data moves between devices by JAX's collectives and lax.ppermute only.
A program may use at most 64 MiB of HBM per device.

v0:
```python
import jax
import jax.numpy as jnp
from jax import lax
from jax.sharding import PartitionSpec as P


first_decay = 0.9
second_decay = 0.999
learn_rate = 0.15
epsilon_term = 0.0001
first_fix = 1.0 - 0.9**10
second_fix = 1.0 - 0.999**10


def silu_parts(inputs):
    sigmoid_part = jax.nn.sigmoid(inputs)
    silu_slope = sigmoid_part * (1.0 + inputs * (1.0 - sigmoid_part))
    silu_bend = sigmoid_part * (1.0 - sigmoid_part) * (2.0 + inputs * (1.0 - 2.0 * sigmoid_part))
    return (silu_slope, silu_bend)


def adahessian(weight, mean_old, curve_old, gradient, probe_value, product):
    diagonal = probe_value.astype(jnp.float32) * product
    mean_new = first_decay * mean_old + (1.0 - first_decay) * gradient
    curve_new = second_decay * curve_old + (1.0 - second_decay) * diagonal * diagonal
    step_ratio = mean_new / first_fix / (jnp.sqrt(curve_new / second_fix) + epsilon_term)
    weight_new = (weight.astype(jnp.float32) - learn_rate * step_ratio).astype(jnp.bfloat16)
    return (weight_new, mean_new, curve_new)


DP = ("z", "c")
MP = ("x", "y")


def chip_ring(x, n_dp):
    n_chip = n_dp // 2
    d = lax.axis_index(DP)
    z = d // 2
    c = d % 2
    partner = [(i, i ^ 1) for i in range(n_dp)]
    ring = [(2 * j, 2 * ((j + 1) % n_chip)) for j in range(n_chip)] + [
        (2 * j + 1, 2 * ((j - 1) % n_chip) + 1) for j in range(n_chip)
    ]
    px = lax.ppermute(x, DP, partner)
    cur = jnp.concatenate([x, px], 0)
    blocks = [(cur, d, d ^ 1)]
    step = 2 * c - 1
    for k in range(1, n_chip // 2 + 1):
        cur = lax.ppermute(cur, DP, ring)
        j = (z + k * step) % n_chip
        blocks.append((cur, 2 * j + c, 2 * j + 1 - c))
        if k < n_chip // 2:
            ex = lax.ppermute(cur, DP, partner)
            j2 = (z - k * step) % n_chip
            blocks.append((ex, 2 * j2 + 1 - c, 2 * j2 + c))
    return blocks


def step(
    tokens, hidden_grad, gate_weight, up_weight, gate_probe, gate_mean, gate_curve, group_counts
):
    n_dp = lax.axis_size(DP)
    n_mp = lax.axis_size(MP)
    rows_loc, feat = tokens.shape
    shard = feat // n_dp
    width = gate_weight.shape[1]
    d = lax.axis_index(DP)

    t3 = tokens.reshape(rows_loc, n_dp, shard)
    a2a = lax.all_to_all(t3, DP, split_axis=1, concat_axis=1, tiled=True)
    pack = jnp.concatenate([tokens, a2a.reshape(rows_loc, feat)], 0)
    gathered = lax.all_gather(pack, MP, axis=0, tiled=False)
    whole = gathered[:, :rows_loc, :].reshape(n_mp * rows_loc, feat)
    group_rows = whole.shape[0]
    cols = (
        gathered[:, rows_loc:, :]
        .reshape(n_mp, rows_loc, n_dp, shard)
        .transpose(2, 0, 1, 3)
        .reshape(n_dp * group_rows, shard)
    )

    w3 = jnp.concatenate([gate_weight, up_weight, gate_probe], 1)
    pre = None
    for block, s0, s1 in chip_ring(w3, n_dp):
        part = jnp.concatenate(
            [
                lax.dynamic_slice_in_dim(whole, s0 * shard, shard, axis=1),
                lax.dynamic_slice_in_dim(whole, s1 * shard, shard, axis=1),
            ],
            1,
        )
        term = jnp.dot(part, block, preferred_element_type=jnp.float32)
        pre = term if pre is None else pre + term
    gate_pre = pre[:, :width]
    up_pre = pre[:, width : 2 * width]
    gate_tan = pre[:, 2 * width :]

    limit = lax.dynamic_index_in_dim(group_counts, d, 0, keepdims=False)
    live = (jnp.arange(group_rows, dtype=jnp.int32) < limit).astype(jnp.float32)
    silu_slope, silu_bend = silu_parts(gate_pre)
    masked = hidden_grad.astype(jnp.float32) * live[:, None]
    grad_gate = (masked * up_pre * silu_slope).astype(jnp.bfloat16)
    tan_gate = (masked * up_pre * silu_bend * gate_tan).astype(jnp.bfloat16)
    packed = jnp.concatenate([grad_gate, tan_gate], 1)

    sums_t = lax.dot_general(
        lax.all_gather(packed, DP, axis=0, tiled=True),
        cols,
        (((0,), (0,)), ((), ())),
        preferred_element_type=jnp.float32,
    )
    gate_out = adahessian(
        gate_weight, gate_mean, gate_curve, sums_t[:width].T, gate_probe, sums_t[width:].T
    )
    return (gate_out[0], gate_out[1], gate_out[2])


def solution(mesh):
    n_dp, n_mp = mesh.devices.shape
    n_x = len({dev.coords[0] for dev in mesh.devices[0]})
    mesh4 = jax.sharding.Mesh(
        mesh.devices.reshape(n_dp // 2, 2, n_x, n_mp // n_x), ("z", "c", "x", "y")
    )
    every = DP + MP
    return jax.shard_map(
        step,
        mesh=mesh4,
        in_specs=(
            P(every, None),
            P(DP, MP),
            P(DP, MP),
            P(DP, MP),
            P(DP, MP),
            P(DP, MP),
            P(DP, MP),
            P(),
        ),
        out_specs=(P(DP, MP), P(DP, MP), P(DP, MP)),
        check_vma=False,
    )
```

profile of v0, /device:TPU:1, one launch (start us, length us, event | category | flops | bytes accessed | tf_op | source)
XLA Modules:
  0.0 196.3 jit_solution(5831661009744188205)
XLA Ops:
  7.2 0.0 all-gather.6.cloned.1.call-start
  7.2 19.2 %all_to_all.5 = bf16[4,16,256]{2,0,1:T(4,128)(2,1)S(1)} all-to-all(bf16[4,16,256]{2,0,1:T(4,128)(2,1)} %bitcast.29), channel_id=1, replica_groups=mesh['z'=8,'c'=2,'x'=4,'y'=8] {'z','c'}, dimensions={1} | all-to-all | bytes 65536 | tf_op jit(solution)/shard_map/all_to_all | solution.py:70
  26.4 1.4 pad_maximum_fusion.2
  27.8 0.0 all-gather.6.cloned.1.call-update
  27.9 0.0 all-gather.4.cloned.1.call-start
  27.9 1.0 constant_dynamic-update-slice_fusion.2
  28.9 1.0 constant_dynamic-update-slice_fusion.1
  29.8 1.0 constant_dynamic-update-slice_fusion
  30.8 0.0 copy-start
  30.8 0.0 copy-start.9
  30.8 2.4 %collective-permute-start = (bf16[256,1344]{0,1:T(8,128)(2,1)S(1)}, bf16[256,1344]{0,1:T(8,128)(2,1)S(1)}, u32[]{:S(2)}, u32[]{:S(2)}) collective-permute-start(bf16[256,1344]{0,1:T(8,128)(2,1)S(1)} %constant_dynamic-update-slice_fusion), channel_id=1, source_target_pairs={{0,32},{32,0},{64,96},{96,64},{128,160},{160,128},{192,224},{224,1... | collective-permute-start | bytes 2064392 | tf_op jit(solution)/shard_map/ppermute | solution.py:44
  33.3 1.7 collective-permute-done
  35.0 0.1 pad_maximum_fusion
  35.1 0.0 copy-done
  35.1 0.7 copy-done.2
  35.9 2.1 %collective-permute-start.1 = (bf16[512,1344]{0,1:T(8,128)(2,1)S(1)}, bf16[512,1344]{0,1:T(8,128)(2,1)}, u32[]{:S(2)}, u32[]{:S(2)}) collective-permute-start(bf16[512,1344]{0,1:T(8,128)(2,1)S(1)} %pad_maximum_fusion), channel_id=1, source_target_pairs={{0,64},{64,128},{128,192},{192,256},{256,320},{320,384},{384,448},... | collective-permute-start | bytes 4128776 | tf_op jit(solution)/shard_map/ppermute | solution.py:49
  38.0 17.3 %collective-permute-done.1 = bf16[512,1344]{0,1:T(8,128)(2,1)} collective-permute-done((bf16[512,1344]{0,1:T(8,128)(2,1)S(1)}, bf16[512,1344]{0,1:T(8,128)(2,1)}, u32[]{:S(2)}, u32[]{:S(2)}) %collective-permute-start.1) | collective-permute-done | bytes 1376288 | tf_op jit(solution)/shard_map/ppermute | solution.py:49
  55.3 3.1 %collective-permute-start.3 = (bf16[512,1344]{0,1:T(8,128)(2,1)}, bf16[512,1344]{0,1:T(8,128)(2,1)}, u32[]{:S(2)}, u32[]{:S(2)}) collective-permute-start(bf16[512,1344]{0,1:T(8,128)(2,1)} %collective-permute-done.1), channel_id=1, source_target_pairs={{0,64},{64,128},{128,192},{192,256},{256,320},{320,384},{384,448},... | collective-permute-start | bytes 4128776 | tf_op jit(solution)/shard_map/ppermute | solution.py:49
  58.6 0.0 copy-done.9
  58.6 0.6 dynamic_slice.52
  59.2 0.6 compare_convert_fusion
  59.9 3.2 %collective-permute-start.2 = (bf16[512,1344]{0,1:T(8,128)(2,1)}, bf16[512,1344]{0,1:T(8,128)(2,1)}, u32[]{:S(2)}, u32[]{:S(2)}) collective-permute-start(bf16[512,1344]{0,1:T(8,128)(2,1)} %collective-permute-done.1), channel_id=1, source_target_pairs={{0,32},{32,0},{64,96},{96,64},{128,160},{160,128},{192,224},{224,1... | collective-permute-start | bytes 4128776 | tf_op jit(solution)/shard_map/ppermute | solution.py:53
  63.1 11.9 %collective-permute-done.3 = bf16[512,1344]{0,1:T(8,128)(2,1)} collective-permute-done((bf16[512,1344]{0,1:T(8,128)(2,1)}, bf16[512,1344]{0,1:T(8,128)(2,1)}, u32[]{:S(2)}, u32[]{:S(2)}) %collective-permute-start.3) | collective-permute-done | bytes 1376288 | tf_op jit(solution)/shard_map/ppermute | solution.py:49
  75.0 4.0 %collective-permute-start.5 = (bf16[512,1344]{0,1:T(8,128)(2,1)}, bf16[512,1344]{0,1:T(8,128)(2,1)}, u32[]{:S(2)}, u32[]{:S(2)}) collective-permute-start(bf16[512,1344]{0,1:T(8,128)(2,1)} %collective-permute-done.3), channel_id=1, source_target_pairs={{0,64},{64,128},{128,192},{192,256},{256,320},{320,384},{384,448},... | collective-permute-start | bytes 4128776 | tf_op jit(solution)/shard_map/ppermute | solution.py:49
  78.9 4.4 %collective-permute-start.4 = (bf16[512,1344]{0,1:T(8,128)(2,1)}, bf16[512,1344]{0,1:T(8,128)(2,1)}, u32[]{:S(2)}, u32[]{:S(2)}) collective-permute-start(bf16[512,1344]{0,1:T(8,128)(2,1)} %collective-permute-done.3), channel_id=1, source_target_pairs={{0,32},{32,0},{64,96},{96,64},{128,160},{160,128},{192,224},{224,1... | collective-permute-start | bytes 4128776 | tf_op jit(solution)/shard_map/ppermute | solution.py:53
  83.3 20.2 %all-gather.6.cloned.1.call-done = bf16[256,4096]{1,0:T(8,128)(2,1)} async-done(((bf16[8,4096]{1,0:T(8,128)(2,1)}), bf16[256,4096]{1,0:T(8,128)(2,1)}) %all-gather.6.cloned.1.call-update) | async-done | bytes 2097168 | tf_op jit(solution)/shard_map/all_gather | solution.py:72
  103.6 3.1 %fusion.53 = (bf16[32,4,4096]{2,1,0:T(4,128)(2,1)S(1)}, bf16[32,4,4096]{2,1,0:T(4,128)(2,1)S(1)}) fusion(bf16[32,8,4096]{2,1,0:T(8,128)(2,1)} %bitcast.28), kind=kLoop, calls=%fused_computation.86 | loop fusion | bytes 4194304 | tf_op jit(solution)/shard_map/slice | solution.py:76
  106.6 0.3 reshape.28
  106.9 0.2 constant_dynamic-slice_fusion.3
  107.1 1.9 fusion.18
  109.0 0.0 copy-start.1
  109.0 0.0 copy-start.3
  109.0 0.0 collective-permute-done.5
  109.0 5.5 %collective-permute-start.7 = (bf16[512,1344]{0,1:T(8,128)(2,1)}, bf16[512,1344]{0,1:T(8,128)(2,1)S(1)}, u32[]{:S(2)}, u32[]{:S(2)}) collective-permute-start(bf16[512,1344]{0,1:T(8,128)(2,1)} %collective-permute-done.5), channel_id=1, source_target_pairs={{0,64},{64,128},{128,192},{192,256},{256,320},{320,384},{384,448},... | collective-permute-start | bytes 4128776 | tf_op jit(solution)/shard_map/ppermute | solution.py:49
  114.5 1.8 fusion.25
  116.4 4.6 %collective-permute-start.6 = (bf16[512,1344]{0,1:T(8,128)(2,1)}, bf16[512,1344]{0,1:T(8,128)(2,1)S(1)}, u32[]{:S(2)}, u32[]{:S(2)}) collective-permute-start(bf16[512,1344]{0,1:T(8,128)(2,1)} %collective-permute-done.5), channel_id=1, source_target_pairs={{0,32},{32,0},{64,96},{96,64},{128,160},{160,128},{192,224},{224,1... | collective-permute-start | bytes 4128776 | tf_op jit(solution)/shard_map/ppermute | solution.py:53
  121.0 0.0 copy-done.1
  121.0 0.0 copy-done.3
  121.0 0.5 convolution_add_fusion.3
  121.5 0.0 collective-permute-done.2
  121.5 1.9 fusion.2
  123.4 1.9 fusion.32
  125.3 0.0 collective-permute-done.4
  125.3 1.9 fusion.1
  127.2 2.9 %collective-permute-done.7 = bf16[512,1344]{0,1:T(8,128)(2,1)S(1)} collective-permute-done((bf16[512,1344]{0,1:T(8,128)(2,1)}, bf16[512,1344]{0,1:T(8,128)(2,1)S(1)}, u32[]{:S(2)}, u32[]{:S(2)}) %collective-permute-start.7) | collective-permute-done | bytes 1376288 | tf_op jit(solution)/shard_map/ppermute | solution.py:49
  130.1 0.5 fusion.39
  130.6 0.0 collective-permute-done.6
  130.6 0.0 copy-start.8
  130.6 0.5 fusion
  131.2 0.4 copy-done.8
  131.5 0.2 fusion.10
  131.7 0.7 pad_maximum_fusion.1
  132.4 0.0 all-gather.4.cloned.1.call-update
  132.4 0.8 reshape.32
  133.2 0.5 copy.14
  133.8 0.3 reshape.30
  134.1 0.0 copy-start.4
  134.1 0.0 copy-start.5
  134.1 0.0 copy-start.6
  134.1 0.0 copy-start.7
  134.1 50.9 %all-gather.4.cloned.1.call-done = bf16[2048,896]{0,1:T(8,128)(2,1)} async-done(((bf16[128,896]{0,1:T(8,128)(2,1)}), bf16[2048,896]{0,1:T(8,128)(2,1)}) %all-gather.4.cloned.1.call-update) | async-done | bytes 3670032 | tf_op jit(solution)/shard_map/all_gather | solution.py:107
  185.0 3.1 %fusion.54 = f32[896,256]{1,0:T(8,128)S(1)} fusion(bf16[2048,896]{0,1:T(8,128)(2,1)} %all-gather.4.cloned.1.call-done, bf16[2048,256]{1,0:T(8,128)(2,1)S(1)} %reshape.30), kind=kOutput, calls=%fused_computation.87 | convolution fusion | flops 939524096 | bytes 5636096 | tf_op jit(solution)/shard_map/dot_general | solution.py:106
  188.1 0.0 copy-done.4
  188.2 1.2 subtract_convert_fusion
  (4 shorter events, 0.0 us)
Async XLA Ops:
  7.2 96.4 %all-gather.6.cloned.1.call-start = ((), (), s32[]{:S(2)}) async-start(), calls=%async_computation.2 | async-start | bytes 2162688 | tf_op jit(solution)/shard_map/all_gather | solution.py:72
  27.9 157.1 %all-gather.4.cloned.1.call-start = ((), (), s32[]{:S(2)}) async-start(), calls=%async_computation.1 | async-start | bytes 3899392 | tf_op jit(solution)/shard_map/all_gather | solution.py:107
  30.8 4.3 %copy-start = (bf16[256,1344]{0,1:T(8,128)(2,1)}, bf16[256,1344]{0,1:T(8,128)(2,1)S(1)}, u32[]{:S(2)}) copy-start(bf16[256,1344]{0,1:T(8,128)(2,1)S(1)} %constant_dynamic-update-slice_fusion) | copy-start | bytes 2064388
  30.8 27.8 %copy-start.9 = (s32[16]{0:T(128)S(1)}, s32[16]{0:T(128)}, u32[]{:S(2)}) copy-start(s32[16]{0:T(128)} %param.15) | copy-start | bytes 196
  30.8 4.2 %collective-permute-start = (bf16[256,1344]{0,1:T(8,128)(2,1)S(1)}, bf16[256,1344]{0,1:T(8,128)(2,1)S(1)}, u32[]{:S(2)}, u32[]{:S(2)}) collective-permute-start(bf16[256,1344]{0,1:T(8,128)(2,1)S(1)} %constant_dynamic-update-slice_fusion), channel_id=1, source_target_pairs={{0,32},{32,0},{64,96},{96,64},{128,160},{160,128},{192,224},{224,1... | collective-permute-start | bytes 2064392 | tf_op jit(solution)/shard_map/ppermute | solution.py:44
  35.0 0.9 copy-start.2
  35.9 19.4 %collective-permute-start.1 = (bf16[512,1344]{0,1:T(8,128)(2,1)S(1)}, bf16[512,1344]{0,1:T(8,128)(2,1)}, u32[]{:S(2)}, u32[]{:S(2)}) collective-permute-start(bf16[512,1344]{0,1:T(8,128)(2,1)S(1)} %pad_maximum_fusion), channel_id=1, source_target_pairs={{0,64},{64,128},{128,192},{192,256},{256,320},{320,384},{384,448},... | collective-permute-start | bytes 4128776 | tf_op jit(solution)/shard_map/ppermute | solution.py:49
  55.3 19.7 %collective-permute-start.3 = (bf16[512,1344]{0,1:T(8,128)(2,1)}, bf16[512,1344]{0,1:T(8,128)(2,1)}, u32[]{:S(2)}, u32[]{:S(2)}) collective-permute-start(bf16[512,1344]{0,1:T(8,128)(2,1)} %collective-permute-done.1), channel_id=1, source_target_pairs={{0,64},{64,128},{128,192},{192,256},{256,320},{320,384},{384,448},... | collective-permute-start | bytes 4128776 | tf_op jit(solution)/shard_map/ppermute | solution.py:49
  59.9 61.7 %collective-permute-start.2 = (bf16[512,1344]{0,1:T(8,128)(2,1)}, bf16[512,1344]{0,1:T(8,128)(2,1)}, u32[]{:S(2)}, u32[]{:S(2)}) collective-permute-start(bf16[512,1344]{0,1:T(8,128)(2,1)} %collective-permute-done.1), channel_id=1, source_target_pairs={{0,32},{32,0},{64,96},{96,64},{128,160},{160,128},{192,224},{224,1... | collective-permute-start | bytes 4128776 | tf_op jit(solution)/shard_map/ppermute | solution.py:53
  75.0 34.1 %collective-permute-start.5 = (bf16[512,1344]{0,1:T(8,128)(2,1)}, bf16[512,1344]{0,1:T(8,128)(2,1)}, u32[]{:S(2)}, u32[]{:S(2)}) collective-permute-start(bf16[512,1344]{0,1:T(8,128)(2,1)} %collective-permute-done.3), channel_id=1, source_target_pairs={{0,64},{64,128},{128,192},{192,256},{256,320},{320,384},{384,448},... | collective-permute-start | bytes 4128776 | tf_op jit(solution)/shard_map/ppermute | solution.py:49
  78.9 46.3 %collective-permute-start.4 = (bf16[512,1344]{0,1:T(8,128)(2,1)}, bf16[512,1344]{0,1:T(8,128)(2,1)}, u32[]{:S(2)}, u32[]{:S(2)}) collective-permute-start(bf16[512,1344]{0,1:T(8,128)(2,1)} %collective-permute-done.3), channel_id=1, source_target_pairs={{0,32},{32,0},{64,96},{96,64},{128,160},{160,128},{192,224},{224,1... | collective-permute-start | bytes 4128776 | tf_op jit(solution)/shard_map/ppermute | solution.py:53
  109.0 12.0 %copy-start.1 = (bf16[256,1344]{0,1:T(8,128)(2,1)S(1)}, bf16[256,1344]{0,1:T(8,128)(2,1)}, u32[]{:S(2)}) copy-start(bf16[256,1344]{0,1:T(8,128)(2,1)} %copy-done) | copy-start | bytes 2064388
  109.0 12.0 %copy-start.3 = (bf16[256,1344]{0,1:T(8,128)(2,1)S(1)}, bf16[256,1344]{0,1:T(8,128)(2,1)}, u32[]{:S(2)}) copy-start(bf16[256,1344]{0,1:T(8,128)(2,1)} %copy-done.2) | copy-start | bytes 2064388
  109.0 21.1 %collective-permute-start.7 = (bf16[512,1344]{0,1:T(8,128)(2,1)}, bf16[512,1344]{0,1:T(8,128)(2,1)S(1)}, u32[]{:S(2)}, u32[]{:S(2)}) collective-permute-start(bf16[512,1344]{0,1:T(8,128)(2,1)} %collective-permute-done.5), channel_id=1, source_target_pairs={{0,64},{64,128},{128,192},{192,256},{256,320},{320,384},{384,448},... | collective-permute-start | bytes 4128776 | tf_op jit(solution)/shard_map/ppermute | solution.py:49
  116.4 14.2 %collective-permute-start.6 = (bf16[512,1344]{0,1:T(8,128)(2,1)}, bf16[512,1344]{0,1:T(8,128)(2,1)S(1)}, u32[]{:S(2)}, u32[]{:S(2)}) collective-permute-start(bf16[512,1344]{0,1:T(8,128)(2,1)} %collective-permute-done.5), channel_id=1, source_target_pairs={{0,32},{32,0},{64,96},{96,64},{128,160},{160,128},{192,224},{224,1... | collective-permute-start | bytes 4128776 | tf_op jit(solution)/shard_map/ppermute | solution.py:53
  130.6 0.9 copy-start.8
  134.1 54.1 %copy-start.4 = (bf16[256,448]{0,1:T(8,128)(2,1)S(1)}, bf16[256,448]{0,1:T(8,128)(2,1)}, u32[]{:S(2)}) copy-start(bf16[256,448]{0,1:T(8,128)(2,1)} %param.10) | copy-start | bytes 688132
  134.1 54.1 %copy-start.5 = (bf16[256,448]{0,1:T(8,128)(2,1)S(1)}, bf16[256,448]{0,1:T(8,128)(2,1)}, u32[]{:S(2)}) copy-start(bf16[256,448]{0,1:T(8,128)(2,1)} %param.12) | copy-start | bytes 688132
  134.1 54.1 %copy-start.6 = (f32[256,448]{0,1:T(8,128)S(1)}, f32[256,448]{0,1:T(8,128)}, u32[]{:S(2)}) copy-start(f32[256,448]{0,1:T(8,128)} %param.13) | copy-start | bytes 1376260
  134.1 54.1 %copy-start.7 = (f32[256,448]{0,1:T(8,128)S(1)}, f32[256,448]{0,1:T(8,128)}, u32[]{:S(2)}) copy-start(f32[256,448]{0,1:T(8,128)} %param.14) | copy-start | bytes 1376260
Sparse Core Ops, SparseCore 0:
  28.0 75.5 all-gather.5
  132.6 52.3 all-gather.3
where the time goes:
time: 197 us; the launch traced here: 196 us
  waiting for transfers between devices  105 us (53%)
  starting transfers between devices  29.3 us (15%)
  blocking collectives  19.2 us (10%)
  between operations  14.6 us (7%)
  matrix products  14 us (7%)
  local copies, waits for them, and re-layouts  9.76 us (5%)
  other arithmetic  4.3 us (2%)
    all_gather x1, waiting for transfers between devices, step(): lax.all_gather(packed, DP, axis=0, tiled=True)  50.9 us
    ppermute x4, waiting for transfers between devices, chip_ring(): cur = lax.ppermute(cur, DP, ring)  32.1 us
    all_gather x1, waiting for transfers between devices, step(): gathered = lax.all_gather(pack, MP, axis=0, tiled=False)  20.2 us
    all_to_all x1, blocking collectives, step(): a2a = lax.all_to_all(t3, DP, split_axis=1, concat_axis=1, tiled=True)  19.2 us
    ppermute x4, starting transfers between devices, chip_ring(): cur = lax.ppermute(cur, DP, ring)  14.7 us
    ppermute x3, starting transfers between devices, chip_ring(): ex = lax.ppermute(cur, DP, partner)  12.1 us
    dot_general x8, matrix products, step(): term = jnp.dot(part, block, preferred_element_type=jnp.float32)  10.9 us
  transfers between devices with their start and end apart: 10, of which 6 were waited for; matrix products, arithmetic and copies ran while one was open for 10% of the time, Pallas kernels for 0%

commit v1 on v0

--- a/solution.py
+++ b/solution.py
@@ -81,15 +81,14 @@
 
     w3 = jnp.concatenate([gate_weight, up_weight, gate_probe], 1)
     pre = None
-    for block, s0, s1 in chip_ring(w3, n_dp):
+    blocks = chip_ring(w3, n_dp)
+    for i in range(0, len(blocks), 2):
+        pair = jnp.concatenate([blocks[i][0], blocks[i + 1][0]], 0)
+        shards = (blocks[i][1], blocks[i][2], blocks[i + 1][1], blocks[i + 1][2])
         part = jnp.concatenate(
-            [
-                lax.dynamic_slice_in_dim(whole, s0 * shard, shard, axis=1),
-                lax.dynamic_slice_in_dim(whole, s1 * shard, shard, axis=1),
-            ],
-            1,
+            [lax.dynamic_slice_in_dim(whole, s * shard, shard, axis=1) for s in shards], 1
         )
-        term = jnp.dot(part, block, preferred_element_type=jnp.float32)
+        term = jnp.dot(part, pair, preferred_element_type=jnp.float32)
         pre = term if pre is None else pre + term
     gate_pre = pre[:, :width]
     up_pre = pre[:, width : 2 * width]

time: 197 us -> 188 us (0.954)
  blocking collectives: 19.2 us -> 0 us
  starting transfers between devices: 29.3 us -> 40.9 us
    all_to_all x1 -> x0, blocking collectives: 19.2 us -> none  [step(): a2a = lax.all_to_all(t3, DP, split_axis=1, concat_axis=1, tiled=True)]
    ppermute x1, starting transfers between devices: 2.43 us -> 8.75 us  [chip_ring(): px = lax.ppermute(x, DP, partner)]
    all_gather x1, waiting for transfers between devices: 20.2 us -> 14.9 us  [step(): gathered = lax.all_gather(pack, MP, axis=0, tiled=False)]
    all_to_all x0 -> x1, starting transfers between devices: none -> 5.11 us  [step(): a2a = lax.all_to_all(t3, DP, split_axis=1, concat_axis=1, tiled=True)]
    ppermute x4, waiting for transfers between devices: 32.1 us -> 37 us  [chip_ring(): cur = lax.ppermute(cur, DP, ring)]
    all_to_all x0 -> x1, waiting for transfers between devices: none -> 2.73 us  [step(): a2a = lax.all_to_all(t3, DP, split_axis=1, concat_axis=1, tiled=True)]
    ppermute x4, starting transfers between devices: 14.7 us -> 16.6 us  [chip_ring(): cur = lax.ppermute(cur, DP, ring)]
    dot_general x8 -> x4, matrix products: 10.9 us -> 10.6 us  [step(): term = jnp.dot(part, pair, preferred_element_type=jnp.float32)]
  transfers between devices with their start and end apart: 10 -> 11, of which waited for: 6 -> 6; matrix products, arithmetic and copies ran while one was open for 10% -> 8% of each run, Pallas kernels for 0% -> 0%
where the time goes in v1:
time: 188 us; the launch traced here: 187 us
  waiting for transfers between devices  106 us (56%)
  starting transfers between devices  40.9 us (22%)
  between operations  14.6 us (8%)
  matrix products  13.8 us (7%)
  local copies, waits for them, and re-layouts  8.97 us (5%)
  other arithmetic  3.54 us (2%)
    all_gather x1, waiting for transfers between devices, step(): lax.all_gather(packed, DP, axis=0, tiled=True)  51 us
    ppermute x4, waiting for transfers between devices, chip_ring(): cur = lax.ppermute(cur, DP, ring)  37 us
    ppermute x4, starting transfers between devices, chip_ring(): cur = lax.ppermute(cur, DP, ring)  16.6 us
    all_gather x1, waiting for transfers between devices, step(): gathered = lax.all_gather(pack, MP, axis=0, tiled=False)  14.9 us
    dot_general x4, matrix products, step(): term = jnp.dot(part, pair, preferred_element_type=jnp.float32)  10.6 us
    ppermute x3, starting transfers between devices, chip_ring(): ex = lax.ppermute(cur, DP, partner)  10.3 us
    ppermute x1, starting transfers between devices, chip_ring(): px = lax.ppermute(x, DP, partner)  8.75 us
    all_to_all x1, starting transfers between devices, step(): a2a = lax.all_to_all(t3, DP, split_axis=1, concat_axis=1, tiled=True)  5.11 us
  transfers between devices with their start and end apart: 11, of which 6 were waited for; matrix products, arithmetic and copies ran while one was open for 8% of the time, Pallas kernels for 0%

profile of v1, /device:TPU:1, one launch (start us, length us, event | category | flops | bytes accessed | tf_op | source)
XLA Modules:
  0.0 187.5 jit_solution(180205597984287651)
XLA Ops:
  7.2 0.0 copy-start.6
  7.2 0.0 copy-start.8
  7.2 1.0 constant_dynamic-update-slice_fusion.2
  8.2 1.0 constant_dynamic-update-slice_fusion.1
  9.1 1.0 constant_dynamic-update-slice_fusion
  10.1 0.0 copy-start
  10.1 8.7 %collective-permute-start = (bf16[256,1344]{0,1:T(8,128)(2,1)S(1)}, bf16[256,1344]{0,1:T(8,128)(2,1)S(1)}, u32[]{:S(2)}, u32[]{:S(2)}) collective-permute-start(bf16[256,1344]{0,1:T(8,128)(2,1)S(1)} %constant_dynamic-update-slice_fusion), channel_id=1, source_target_pairs={{0,32},{32,0},{64,96},{96,64},{128,160},{160,128},{192,224},{224,1... | collective-permute-start | bytes 2064392 | tf_op jit(solution)/shard_map/ppermute | solution.py:44
  18.8 5.1 %all-to-all-start = ((bf16[4,16,256]{2,0,1:T(4,128)(2,1)}), bf16[4,16,256]{2,0,1:T(4,128)(2,1)S(1)}, u32[]{:S(2)}, u32[]{:S(2)}) async-start(bf16[4,16,256]{2,0,1:T(4,128)(2,1)} %bitcast.22), calls=%async_computation | async-start | bytes 65536 | tf_op jit(solution)/shard_map/all_to_all | solution.py:70
  23.9 0.0 all-gather.6.cloned.1.call-start
  24.0 0.0 collective-permute-done
  24.0 0.0 copy-start.3
  24.0 0.1 pad_maximum_fusion
  24.1 4.5 %collective-permute-start.1 = (bf16[512,1344]{0,1:T(8,128)(2,1)S(1)}, bf16[512,1344]{0,1:T(8,128)(2,1)}, u32[]{:S(2)}, u32[]{:S(2)}) collective-permute-start(bf16[512,1344]{0,1:T(8,128)(2,1)S(1)} %pad_maximum_fusion), channel_id=1, source_target_pairs={{0,64},{64,128},{128,192},{192,256},{256,320},{320,384},{384,448},... | collective-permute-start | bytes 4128776 | tf_op jit(solution)/shard_map/ppermute | solution.py:49
  28.6 2.7 %all-to-all-done = bf16[4,16,256]{2,0,1:T(4,128)(2,1)S(1)} async-done(((bf16[4,16,256]{2,0,1:T(4,128)(2,1)}), bf16[4,16,256]{2,0,1:T(4,128)(2,1)S(1)}, u32[]{:S(2)}, u32[]{:S(2)}) %all-to-all-start) | async-done | bytes 32800 | tf_op jit(solution)/shard_map/all_to_all | solution.py:70
  31.3 0.0 copy-done.6
  31.3 0.7 pad_maximum_fusion.2
  32.0 0.0 all-gather.6.cloned.1.call-update
  32.0 0.0 all-gather.4.cloned.1.call-start
  32.1 11.8 %collective-permute-done.1 = bf16[512,1344]{0,1:T(8,128)(2,1)} collective-permute-done((bf16[512,1344]{0,1:T(8,128)(2,1)S(1)}, bf16[512,1344]{0,1:T(8,128)(2,1)}, u32[]{:S(2)}, u32[]{:S(2)}) %collective-permute-start.1) | collective-permute-done | bytes 1376288 | tf_op jit(solution)/shard_map/ppermute | solution.py:49
  43.8 5.1 %collective-permute-start.3 = (bf16[512,1344]{0,1:T(8,128)(2,1)}, bf16[512,1344]{0,1:T(8,128)(2,1)}, u32[]{:S(2)}, u32[]{:S(2)}) collective-permute-start(bf16[512,1344]{0,1:T(8,128)(2,1)} %collective-permute-done.1), channel_id=1, source_target_pairs={{0,64},{64,128},{128,192},{192,256},{256,320},{320,384},{384,448},... | collective-permute-start | bytes 4128776 | tf_op jit(solution)/shard_map/ppermute | solution.py:49
  49.0 15.5 %collective-permute-done.3 = bf16[512,1344]{0,1:T(8,128)(2,1)} collective-permute-done((bf16[512,1344]{0,1:T(8,128)(2,1)}, bf16[512,1344]{0,1:T(8,128)(2,1)}, u32[]{:S(2)}, u32[]{:S(2)}) %collective-permute-start.3) | collective-permute-done | bytes 1376288 | tf_op jit(solution)/shard_map/ppermute | solution.py:49
  64.5 5.1 %collective-permute-start.5 = (bf16[512,1344]{0,1:T(8,128)(2,1)}, bf16[512,1344]{0,1:T(8,128)(2,1)}, u32[]{:S(2)}, u32[]{:S(2)}) collective-permute-start(bf16[512,1344]{0,1:T(8,128)(2,1)} %collective-permute-done.3), channel_id=1, source_target_pairs={{0,64},{64,128},{128,192},{192,256},{256,320},{320,384},{384,448},... | collective-permute-start | bytes 4128776 | tf_op jit(solution)/shard_map/ppermute | solution.py:49
  69.7 0.0 copy-done.8
  69.7 0.6 dynamic_slice.52
  70.3 1.9 %collective-permute-start.2 = (bf16[512,1344]{0,1:T(8,128)(2,1)}, bf16[512,1344]{0,1:T(8,128)(2,1)}, u32[]{:S(2)}, u32[]{:S(2)}) collective-permute-start(bf16[512,1344]{0,1:T(8,128)(2,1)} %collective-permute-done.1), channel_id=1, source_target_pairs={{0,32},{32,0},{64,96},{96,64},{128,160},{160,128},{192,224},{224,1... | collective-permute-start | bytes 4128776 | tf_op jit(solution)/shard_map/ppermute | solution.py:53
  72.2 0.7 compare_convert_fusion
  73.1 2.4 %collective-permute-start.4 = (bf16[512,1344]{0,1:T(8,128)(2,1)}, bf16[512,1344]{0,1:T(8,128)(2,1)}, u32[]{:S(2)}, u32[]{:S(2)}) collective-permute-start(bf16[512,1344]{0,1:T(8,128)(2,1)} %collective-permute-done.3), channel_id=1, source_target_pairs={{0,32},{32,0},{64,96},{96,64},{128,160},{160,128},{192,224},{224,1... | collective-permute-start | bytes 4128776 | tf_op jit(solution)/shard_map/ppermute | solution.py:53
  75.5 9.7 %collective-permute-done.5 = bf16[512,1344]{0,1:T(8,128)(2,1)} collective-permute-done((bf16[512,1344]{0,1:T(8,128)(2,1)}, bf16[512,1344]{0,1:T(8,128)(2,1)}, u32[]{:S(2)}, u32[]{:S(2)}) %collective-permute-start.5) | collective-permute-done | bytes 1376288 | tf_op jit(solution)/shard_map/ppermute | solution.py:49
  85.2 6.0 %collective-permute-start.6 = (bf16[512,1344]{0,1:T(8,128)(2,1)}, bf16[512,1344]{0,1:T(8,128)(2,1)}, u32[]{:S(2)}, u32[]{:S(2)}) collective-permute-start(bf16[512,1344]{0,1:T(8,128)(2,1)} %collective-permute-done.5), channel_id=1, source_target_pairs={{0,32},{32,0},{64,96},{96,64},{128,160},{160,128},{192,224},{224,1... | collective-permute-start | bytes 4128776 | tf_op jit(solution)/shard_map/ppermute | solution.py:53
  91.2 1.9 %collective-permute-start.7 = (bf16[512,1344]{0,1:T(8,128)(2,1)}, bf16[512,1344]{0,1:T(8,128)(2,1)}, u32[]{:S(2)}, u32[]{:S(2)}) collective-permute-start(bf16[512,1344]{0,1:T(8,128)(2,1)} %collective-permute-done.5), channel_id=1, source_target_pairs={{0,64},{64,128},{128,192},{192,256},{256,320},{320,384},{384,448},... | collective-permute-start | bytes 4128776 | tf_op jit(solution)/shard_map/ppermute | solution.py:49
  93.1 14.9 %all-gather.6.cloned.1.call-done = bf16[256,4096]{1,0:T(8,128)(2,1)} async-done(((bf16[8,4096]{1,0:T(8,128)(2,1)}), bf16[256,4096]{1,0:T(8,128)(2,1)}) %all-gather.6.cloned.1.call-update) | async-done | bytes 2097168 | tf_op jit(solution)/shard_map/all_gather | solution.py:72
  108.0 0.0 copy-done
  108.1 0.0 copy-done.3
  108.1 3.4 %fusion.73 = (bf16[32,4,4096]{2,1,0:T(4,128)(2,1)S(1)}, bf16[32,4,4096]{2,1,0:T(4,128)(2,1)S(1)}) fusion(bf16[32,8,4096]{2,1,0:T(8,128)(2,1)} %bitcast.21), kind=kLoop, calls=%fused_computation.96 | loop fusion | bytes 4194304 | tf_op jit(solution)/shard_map/slice | solution.py:76
  111.4 0.3 reshape.28
  111.7 0.2 constant_dynamic-slice_fusion.3
  111.9 2.6 %fusion = f32[128,1344]{0,1:T(8,128)S(1)} fusion(bf16[512,1344]{0,1:T(8,128)(2,1)} %collective-permute-done.1, bf16[256,1344]{0,1:T(8,128)(2,1)} %copy-done.3, bf16[256,1344]{0,1:T(8,128)(2,1)} %copy-done, bf16[128,256]{1,0:T(8,128)(2,1)S(1)} %get-tuple-element.20, bf16[128,256]{1,0:T(8,128)(2,1)S(1)} %get-tuple-element.21, ...), kind=kOutput, calls=%fused_computation | convolution fusion | flops 361627648 | bytes 3702784 | tf_op jit(solution)/shard_map/dot_general | solution.py:91
  114.5 0.0 collective-permute-done.2
  114.6 2.7 %fusion.24 = f32[128,1344]{0,1:T(8,128)S(1)} fusion(f32[128,1344]{0,1:T(8,128)S(1)} %fusion, bf16[512,1344]{0,1:T(8,128)(2,1)} %collective-permute-done.3, bf16[512,1344]{0,1:T(8,128)(2,1)} %collective-permute-done.2, bf16[128,256]{1,0:T(8,128)(2,1)S(1)} %get-tuple-element.16, bf16[128,256]{1,0:T(8,128)(2,1)S(1)} %get-tuple-element.17, ...), kind=kOutput, calls=%fused_computation.20 | convolution fusion | flops 359047168 | bytes 4390912 | tf_op jit(solution)/shard_map/dot_general | solution.py:91
  117.2 0.0 collective-permute-done.4
  117.2 2.7 %fusion.21 = f32[128,1344]{0,1:T(8,128)S(1)} fusion(f32[128,1344]{0,1:T(8,128)S(1)} %fusion.24, bf16[512,1344]{0,1:T(8,128)(2,1)} %collective-permute-done.5, bf16[512,1344]{0,1:T(8,128)(2,1)} %collective-permute-done.4, bf16[128,256]{1,0:T(8,128)(2,1)S(1)} %get-tuple-element.12, bf16[128,256]{1,0:T(8,128)(2,1)S(1)} %get-tuple-element.13, ...), kind=kOutput, calls=%fused_computation.19 | convolution fusion | flops 359047168 | bytes 4390912 | tf_op jit(solution)/shard_map/dot_general | solution.py:91
  119.9 0.0 collective-permute-done.6
  119.9 0.0 collective-permute-done.7
  119.9 0.0 copy-start.7
  119.9 2.7 %fusion.18 = f32[128,1344]{0,1:T(8,128)S(1)} fusion(f32[128,1344]{0,1:T(8,128)S(1)} %fusion.21, bf16[512,1344]{0,1:T(8,128)(2,1)} %collective-permute-done.7, bf16[512,1344]{0,1:T(8,128)(2,1)} %collective-permute-done.6, bf16[128,256]{1,0:T(8,128)(2,1)S(1)} %get-tuple-element.9, bf16[128,256]{1,0:T(8,128)(2,1)S(1)} %get-tuple-element.10, ...), kind=kOutput, calls=%fused_computation.18 | convolution fusion | flops 359047168 | bytes 4390912 | tf_op jit(solution)/shard_map/dot_general | solution.py:91
  122.6 0.0 copy-done.7
  122.6 0.2 fusion.62
  122.8 0.7 pad_maximum_fusion.1
  123.5 0.0 all-gather.4.cloned.1.call-update
  123.5 0.8 reshape.32
  124.3 0.5 copy.14
  124.9 0.3 reshape.30
  125.2 0.0 copy-start.1
  125.2 0.0 copy-start.2
  125.2 0.0 copy-start.4
  125.2 0.0 copy-start.5
  125.2 51.0 %all-gather.4.cloned.1.call-done = bf16[2048,896]{0,1:T(8,128)(2,1)} async-done(((bf16[128,896]{0,1:T(8,128)(2,1)}), bf16[2048,896]{0,1:T(8,128)(2,1)}) %all-gather.4.cloned.1.call-update) | async-done | bytes 3670032 | tf_op jit(solution)/shard_map/all_gather | solution.py:106
  176.2 3.1 %fusion.74 = f32[896,256]{1,0:T(8,128)S(1)} fusion(bf16[2048,896]{0,1:T(8,128)(2,1)} %all-gather.4.cloned.1.call-done, bf16[2048,256]{1,0:T(8,128)(2,1)S(1)} %reshape.30), kind=kOutput, calls=%fused_computation.97 | convolution fusion | flops 939524096 | bytes 5636096 | tf_op jit(solution)/shard_map/dot_general | solution.py:105
  179.3 0.0 copy-done.1
  179.4 0.0 copy-done.2
  179.4 0.0 copy-done.4
  179.4 0.0 copy-done.5
  179.4 1.2 subtract_convert_fusion
Async XLA Ops:
  7.2 24.2 %copy-start.6 = (bf16[4,4096]{1,0:T(4,128)(2,1)S(1)}, bf16[4,4096]{1,0:T(4,128)(2,1)}, u32[]{:S(2)}) copy-start(bf16[4,4096]{1,0:T(4,128)(2,1)} %param.8) | copy-start | bytes 98308
  7.2 62.5 %copy-start.8 = (s32[16]{0:T(128)S(1)}, s32[16]{0:T(128)}, u32[]{:S(2)}) copy-start(s32[16]{0:T(128)} %param.15) | copy-start | bytes 196
  10.1 98.0 %copy-start = (bf16[256,1344]{0,1:T(8,128)(2,1)}, bf16[256,1344]{0,1:T(8,128)(2,1)S(1)}, u32[]{:S(2)}) copy-start(bf16[256,1344]{0,1:T(8,128)(2,1)S(1)} %constant_dynamic-update-slice_fusion) | copy-start | bytes 2064388
  10.1 13.9 %collective-permute-start = (bf16[256,1344]{0,1:T(8,128)(2,1)S(1)}, bf16[256,1344]{0,1:T(8,128)(2,1)S(1)}, u32[]{:S(2)}, u32[]{:S(2)}) collective-permute-start(bf16[256,1344]{0,1:T(8,128)(2,1)S(1)} %constant_dynamic-update-slice_fusion), channel_id=1, source_target_pairs={{0,32},{32,0},{64,96},{96,64},{128,160},{160,128},{192,224},{224,1... | collective-permute-start | bytes 2064392 | tf_op jit(solution)/shard_map/ppermute | solution.py:44
  18.8 12.5 %all-to-all-start = ((bf16[4,16,256]{2,0,1:T(4,128)(2,1)}), bf16[4,16,256]{2,0,1:T(4,128)(2,1)S(1)}, u32[]{:S(2)}, u32[]{:S(2)}) async-start(bf16[4,16,256]{2,0,1:T(4,128)(2,1)} %bitcast.22), calls=%async_computation | async-start | bytes 65536 | tf_op jit(solution)/shard_map/all_to_all | solution.py:70
  23.9 84.1 %all-gather.6.cloned.1.call-start = ((), (), s32[]{:S(2)}) async-start(), calls=%async_computation.2 | async-start | bytes 2162688 | tf_op jit(solution)/shard_map/all_gather | solution.py:72
  24.0 84.1 %copy-start.3 = (bf16[256,1344]{0,1:T(8,128)(2,1)}, bf16[256,1344]{0,1:T(8,128)(2,1)S(1)}, u32[]{:S(2)}) copy-start(bf16[256,1344]{0,1:T(8,128)(2,1)S(1)} %collective-permute-done) | copy-start | bytes 2064388
  24.1 19.7 %collective-permute-start.1 = (bf16[512,1344]{0,1:T(8,128)(2,1)S(1)}, bf16[512,1344]{0,1:T(8,128)(2,1)}, u32[]{:S(2)}, u32[]{:S(2)}) collective-permute-start(bf16[512,1344]{0,1:T(8,128)(2,1)S(1)} %pad_maximum_fusion), channel_id=1, source_target_pairs={{0,64},{64,128},{128,192},{192,256},{256,320},{320,384},{384,448},... | collective-permute-start | bytes 4128776 | tf_op jit(solution)/shard_map/ppermute | solution.py:49
  32.0 144.2 %all-gather.4.cloned.1.call-start = ((), (), s32[]{:S(2)}) async-start(), calls=%async_computation.1 | async-start | bytes 3899392 | tf_op jit(solution)/shard_map/all_gather | solution.py:106
  43.8 20.7 %collective-permute-start.3 = (bf16[512,1344]{0,1:T(8,128)(2,1)}, bf16[512,1344]{0,1:T(8,128)(2,1)}, u32[]{:S(2)}, u32[]{:S(2)}) collective-permute-start(bf16[512,1344]{0,1:T(8,128)(2,1)} %collective-permute-done.1), channel_id=1, source_target_pairs={{0,64},{64,128},{128,192},{192,256},{256,320},{320,384},{384,448},... | collective-permute-start | bytes 4128776 | tf_op jit(solution)/shard_map/ppermute | solution.py:49
  64.5 20.7 %collective-permute-start.5 = (bf16[512,1344]{0,1:T(8,128)(2,1)}, bf16[512,1344]{0,1:T(8,128)(2,1)}, u32[]{:S(2)}, u32[]{:S(2)}) collective-permute-start(bf16[512,1344]{0,1:T(8,128)(2,1)} %collective-permute-done.3), channel_id=1, source_target_pairs={{0,64},{64,128},{128,192},{192,256},{256,320},{320,384},{384,448},... | collective-permute-start | bytes 4128776 | tf_op jit(solution)/shard_map/ppermute | solution.py:49
  70.3 44.3 %collective-permute-start.2 = (bf16[512,1344]{0,1:T(8,128)(2,1)}, bf16[512,1344]{0,1:T(8,128)(2,1)}, u32[]{:S(2)}, u32[]{:S(2)}) collective-permute-start(bf16[512,1344]{0,1:T(8,128)(2,1)} %collective-permute-done.1), channel_id=1, source_target_pairs={{0,32},{32,0},{64,96},{96,64},{128,160},{160,128},{192,224},{224,1... | collective-permute-start | bytes 4128776 | tf_op jit(solution)/shard_map/ppermute | solution.py:53
  73.1 44.2 %collective-permute-start.4 = (bf16[512,1344]{0,1:T(8,128)(2,1)}, bf16[512,1344]{0,1:T(8,128)(2,1)}, u32[]{:S(2)}, u32[]{:S(2)}) collective-permute-start(bf16[512,1344]{0,1:T(8,128)(2,1)} %collective-permute-done.3), channel_id=1, source_target_pairs={{0,32},{32,0},{64,96},{96,64},{128,160},{160,128},{192,224},{224,1... | collective-permute-start | bytes 4128776 | tf_op jit(solution)/shard_map/ppermute | solution.py:53
  85.2 34.7 %collective-permute-start.6 = (bf16[512,1344]{0,1:T(8,128)(2,1)}, bf16[512,1344]{0,1:T(8,128)(2,1)}, u32[]{:S(2)}, u32[]{:S(2)}) collective-permute-start(bf16[512,1344]{0,1:T(8,128)(2,1)} %collective-permute-done.5), channel_id=1, source_target_pairs={{0,32},{32,0},{64,96},{96,64},{128,160},{160,128},{192,224},{224,1... | collective-permute-start | bytes 4128776 | tf_op jit(solution)/shard_map/ppermute | solution.py:53
  91.2 28.7 %collective-permute-start.7 = (bf16[512,1344]{0,1:T(8,128)(2,1)}, bf16[512,1344]{0,1:T(8,128)(2,1)}, u32[]{:S(2)}, u32[]{:S(2)}) collective-permute-start(bf16[512,1344]{0,1:T(8,128)(2,1)} %collective-permute-done.5), channel_id=1, source_target_pairs={{0,64},{64,128},{128,192},{192,256},{256,320},{320,384},{384,448},... | collective-permute-start | bytes 4128776 | tf_op jit(solution)/shard_map/ppermute | solution.py:49
  119.9 2.7 %copy-start.7 = (bf16[128,448]{0,1:T(8,128)(2,1)S(1)}, bf16[128,448]{0,1:T(8,128)(2,1)}, u32[]{:S(2)}) copy-start(bf16[128,448]{0,1:T(8,128)(2,1)} %param.9) | copy-start | bytes 344068
  125.2 54.2 %copy-start.1 = (bf16[256,448]{0,1:T(8,128)(2,1)S(1)}, bf16[256,448]{0,1:T(8,128)(2,1)}, u32[]{:S(2)}) copy-start(bf16[256,448]{0,1:T(8,128)(2,1)} %param.10) | copy-start | bytes 688132
  125.2 54.2 %copy-start.2 = (bf16[256,448]{0,1:T(8,128)(2,1)S(1)}, bf16[256,448]{0,1:T(8,128)(2,1)}, u32[]{:S(2)}) copy-start(bf16[256,448]{0,1:T(8,128)(2,1)} %param.12) | copy-start | bytes 688132
  125.2 54.2 %copy-start.4 = (f32[256,448]{0,1:T(8,128)S(1)}, f32[256,448]{0,1:T(8,128)}, u32[]{:S(2)}) copy-start(f32[256,448]{0,1:T(8,128)} %param.13) | copy-start | bytes 1376260
  125.2 54.2 %copy-start.5 = (f32[256,448]{0,1:T(8,128)S(1)}, f32[256,448]{0,1:T(8,128)}, u32[]{:S(2)}) copy-start(f32[256,448]{0,1:T(8,128)} %param.14) | copy-start | bytes 1376260
Sparse Core Ops, SparseCore 0:
  32.2 75.8 all-gather.5
  123.7 52.4 all-gather.3
